TPU v7x, 32 devices: a whole 2x2x4 slice. The times are simulated.
32 devices in a mesh: blk: 8 (over z, core), vb: 4 (over y, x).
Axes of the slice: x: 2, y: 2, z: 4, core: 2. Of those that a mesh axis runs over, the one named last changes fastest.
Arguments:
- amplitudes: float32 [32, 1024, 1024], P('blk', 'vb'), may hold values from -6 to 6
- integrals: float32 [2048, 1024], P('blk'), may hold values from -0.5 to 0.5
- row_orbitals: int32 [2048], P('blk'), may hold values from 0 to 1023
- pair_orbitals: int32 [32, 2], P('blk'), may hold values from 0 to 255
- occupied_energy: float32 [256], replicated, may hold values from -2 to -0.5
- virtual_energy: float32 [1024], replicated, may hold values from 0.5 to 3
Outputs:
- density: float32 [32, 1024, 1024], P('blk', 'vb')
All inputs are finite; a program needn't handle non-finite values.
Results may differ from a plain program's by a relative error of at most 0.0003.
Values sent between devices are 32-bit elements; how exact they have to be, the bound alone decides.
No kernel may reach another device: no remote copies, remote signals or barrier semaphores. Data moves between devices by JAX's collectives and lax.ppermute only.
A program may use at most 64 MiB of HBM per device.

v0:
```python
import jax
import jax.numpy as jnp
from jax import lax
from jax.sharding import PartitionSpec as P

HOPS = 5


def passed_along(block, axis, distance):
    devices = range(lax.axis_size(axis))
    route = [((i - distance) % len(devices), i) for i in devices]
    return lax.ppermute(block, axis, route)


def step_down(carried):
    return passed_along(carried, "blk", 1)


def local(amplitudes, integrals, row_orbitals, pair_orbitals, occupied_energy, virtual_energy):
    width = virtual_energy.shape[0]
    nocc = occupied_energy.shape[0]
    quarter = width // lax.axis_size("vb")
    qstart = lax.axis_index("vb") * quarter
    virt_iota = jnp.arange(width, dtype=jnp.int32)
    occ_iota = jnp.arange(nocc, dtype=jnp.int32)
    row_energy = jnp.sum(
        jnp.where(row_orbitals[:, None] == virt_iota[None, :], virtual_energy[None, :], 0.0), axis=1
    )
    pair_match = pair_orbitals[:, :, None] == occ_iota[None, None, :]
    pair_energy = jnp.sum(jnp.where(pair_match, occupied_energy[None, None, :], 0.0), axis=(1, 2))
    own_virtual = lax.dynamic_slice_in_dim(virtual_energy, qstart, quarter, 0)
    own = (integrals, row_energy)
    window = [own]
    current = passed_along((own[0], own[1]), "blk", -(HOPS - HOPS // 2))
    window = [current]
    for turn in range(HOPS):
        current = step_down(current)
        window.append(current)
    factors = lax.all_to_all(amplitudes, "vb", split_axis=2, concat_axis=1, tiled=True)

    def pair_columns(inputs):
        factor, energy = inputs
        total = jnp.zeros((width, quarter), jnp.float32)
        for block, energies in window:
            denom = energies[:, None] + own_virtual[None, :] - energy
            weighted = jnp.dot(
                block, factor, precision=lax.Precision.HIGHEST, preferred_element_type=jnp.float32
            )
            total = total + jnp.dot(
                block.T,
                weighted / denom,
                precision=lax.Precision.HIGHEST,
                preferred_element_type=jnp.float32,
            )
        return total

    totals = lax.map(pair_columns, (factors, pair_energy))
    return lax.all_to_all(totals, "vb", split_axis=1, concat_axis=2, tiled=True)


def solution(mesh):
    return jax.shard_map(
        local,
        mesh=mesh,
        in_specs=(P("blk", "vb", None), P("blk", None), P("blk"), P("blk", None), P(), P()),
        out_specs=P("blk", "vb", None),
        check_vma=False,
    )
```

profile of v0, /device:TPU:0, one launch (start us, length us, event | category | flops | bytes accessed | tf_op | source)
XLA Modules:
  0.0 425.2 jit_solution(7205439664500854542)
XLA Ops:
  0.0 3.5 collective-permute-start
  3.5 22.9 %collective-permute-done = f32[256,1024]{1,0:T(8,128)S(1)} collective-permute-done((f32[256,1024]{1,0:T(8,128)}, f32[256,1024]{1,0:T(8,128)S(1)}, u32[]{:S(2)}, u32[]{:S(2)}) %collective-permute-start) | collective-permute-done | bytes 1048608 | tf_op jit(solution)/shard_map/ppermute | solution.py:12
  26.4 12.8 %collective-permute-start.2 = (f32[256,1024]{1,0:T(8,128)S(1)}, f32[256,1024]{1,0:T(8,128)S(1)}, u32[]{:S(2)}, u32[]{:S(2)}) collective-permute-start(f32[256,1024]{1,0:T(8,128)S(1)} %collective-permute-done), channel_id=1, source_target_pairs={{28,0},{0,4},{4,8},{8,12},{12,16},{16,20},{20,24},{24,28},{29,1},{... | collective-permute-start | bytes 3145736 | tf_op jit(solution)/shard_map/ppermute | solution.py:12
  39.2 15.6 %collective-permute-done.2 = f32[256,1024]{1,0:T(8,128)S(1)} collective-permute-done((f32[256,1024]{1,0:T(8,128)S(1)}, f32[256,1024]{1,0:T(8,128)S(1)}, u32[]{:S(2)}, u32[]{:S(2)}) %collective-permute-start.2) | collective-permute-done | bytes 1048608 | tf_op jit(solution)/shard_map/ppermute | solution.py:12
  54.8 5.3 %copy.15 = f32[4,256,1024]{1,0,2:T(4,128)} copy(f32[4,256,1024]{2,1,0:T(8,128)} %param.8) | data formatting | bytes 8388608 | tf_op args[0]
  60.1 5.0 %all-to-all-start = ((f32[4,256,1024]{1,0,2:T(4,128)}), f32[4,256,1024]{1,0,2:T(4,128)}, u32[]{:S(2)}, u32[]{:S(2)}) async-start(f32[4,256,1024]{1,0,2:T(4,128)} %copy.15), calls=%async_computation | async-start | bytes 8388608 | tf_op jit(solution)/shard_map/all_to_all | solution.py:39
  65.1 5.7 %collective-permute-done.4 = f32[256,1024]{1,0:T(8,128)S(1)} collective-permute-done((f32[256,1024]{1,0:T(8,128)S(1)}, f32[256,1024]{1,0:T(8,128)S(1)}, u32[]{:S(2)}, u32[]{:S(2)}) %collective-permute-start.4) | collective-permute-done | bytes 1048608 | tf_op jit(solution)/shard_map/ppermute | solution.py:12
  70.8 16.0 %collective-permute-done.6 = f32[256,1024]{1,0:T(8,128)S(1)} collective-permute-done((f32[256,1024]{1,0:T(8,128)S(1)}, f32[256,1024]{1,0:T(8,128)S(1)}, u32[]{:S(2)}, u32[]{:S(2)}) %collective-permute-start.6) | collective-permute-done | bytes 1048608 | tf_op jit(solution)/shard_map/ppermute | solution.py:12
  86.8 1.1 copy-done.1
  87.9 16.1 %collective-permute-done.8 = f32[256,1024]{1,0:T(8,128)} collective-permute-done((f32[256,1024]{1,0:T(8,128)S(1)}, f32[256,1024]{1,0:T(8,128)}, u32[]{:S(2)}, u32[]{:S(2)}) %collective-permute-start.8) | collective-permute-done | bytes 1048608 | tf_op jit(solution)/shard_map/ppermute | solution.py:12
  104.4 3.0 collective-permute-done.1
  107.4 3.0 collective-permute-start.3
  110.3 10.6 %collective-permute-done.3 = f32[256]{0:T(256)S(1)} collective-permute-done((f32[256]{0:T(256)S(1)}, f32[256]{0:T(256)S(1)}, u32[]{:S(2)}, u32[]{:S(2)}) %collective-permute-start.3) | collective-permute-done | bytes 1056 | tf_op jit(solution)/shard_map/ppermute | solution.py:12
  120.9 4.8 %collective-permute-done.5 = f32[256]{0:T(256)S(1)} collective-permute-done((f32[256]{0:T(256)S(1)}, f32[256]{0:T(256)S(1)}, u32[]{:S(2)}, u32[]{:S(2)}) %collective-permute-start.5) | collective-permute-done | bytes 1056 | tf_op jit(solution)/shard_map/ppermute | solution.py:12
  125.7 4.8 %collective-permute-done.7 = f32[256]{0:T(256)S(1)} collective-permute-done((f32[256]{0:T(256)S(1)}, f32[256]{0:T(256)S(1)}, u32[]{:S(2)}, u32[]{:S(2)}) %collective-permute-start.7) | collective-permute-done | bytes 1056 | tf_op jit(solution)/shard_map/ppermute | solution.py:12
  130.5 4.8 %collective-permute-done.9 = f32[256]{0:T(256)S(1)} collective-permute-done((f32[256]{0:T(256)S(1)}, f32[256]{0:T(256)S(1)}, u32[]{:S(2)}, u32[]{:S(2)}) %collective-permute-start.9) | collective-permute-done | bytes 1056 | tf_op jit(solution)/shard_map/ppermute | solution.py:12
  135.6 5.2 %copy.16 = f32[4,4,256,256]{3,2,1,0:T(8,128)} copy(f32[4,4,256,256]{2,0,3,1:T(4,128)} %bitcast.11) | data formatting | bytes 8388608 | tf_op jit(solution)/shard_map/all_to_all | solution.py:39
  140.8 225.5 %while.10 = (s32[]{:T(128)}, f32[4,1024,256]{2,0,1:T(4,128)}, f32[4,1024,256]{2,1,0:T(8,128)}, f32[256,1024]{1,0:T(8,128)S(1)}, f32[256]{0:T(256)S(1)}, /*index=...) while((s32[]{:T(128)}, f32[4,1024,256]{2,0,1:T(4,128)}, ...), condition=%wide.region_3.4_spmd, body=%wide.region_2.3_spmd.sunk | while | flops 9666166784 | bytes 58733852 | solution.py:57
  141.7 4.1 fusion.100
  146.8 2.5 fusion.102
  149.4 1.0 convolution_add_fusion.9
  150.4 2.5 fusion.103
  154.0 2.5 fusion.104
  157.5 3.7 fusion.105
  161.3 2.3 convolution_add_fusion.12
  163.5 3.7 fusion.106
  167.3 3.2 fusion.107
  170.5 3.6 copy.24
  174.1 23.2 %dynamic_update_slice.5 = f32[4,1024,256]{2,0,1:T(4,128)} dynamic-update-slice(f32[4,1024,256]{2,0,1:T(4,128)} %get-tuple-element.250, f32[1,1024,256]{2,0,1:T(1,128)} %copy.24, s32[]{:T(128)} %get-tuple-element.249, s32[]{:T(128)} %constant.3.clone.1..sunk, s32[]{:T(128)} %constant.3.clone.1..sunk) | dynamic-update-slice | bytes 2097156 | tf_op jit(solution)/shard_map/while/body/jit(dynamic_update_index_in_dim)/dynamic_update_slice | solution.py:57
  198.0 4.1 fusion.100
  203.2 2.5 fusion.102
  206.7 2.5 fusion.103
  210.3 2.5 fusion.104
  213.9 3.7 fusion.105
  217.6 2.3 convolution_add_fusion.12
  219.9 3.7 fusion.106
  223.6 3.2 fusion.107
  226.8 3.6 copy.24
  230.5 23.2 %dynamic_update_slice.5 = f32[4,1024,256]{2,0,1:T(4,128)} dynamic-update-slice(f32[4,1024,256]{2,0,1:T(4,128)} %get-tuple-element.250, f32[1,1024,256]{2,0,1:T(1,128)} %copy.24, s32[]{:T(128)} %get-tuple-element.249, s32[]{:T(128)} %constant.3.clone.1..sunk, s32[]{:T(128)} %constant.3.clone.1..sunk) | dynamic-update-slice | bytes 2097156 | tf_op jit(solution)/shard_map/while/body/jit(dynamic_update_index_in_dim)/dynamic_update_slice | solution.py:57
  254.4 4.1 fusion.100
  259.5 2.5 fusion.102
  262.0 1.0 convolution_add_fusion.9
  263.1 2.5 fusion.103
  266.6 2.5 fusion.104
  270.2 3.7 fusion.105
  273.9 2.3 convolution_add_fusion.12
  276.2 3.7 fusion.106
  279.9 3.2 fusion.107
  283.2 3.6 copy.24
  286.8 23.2 %dynamic_update_slice.5 = f32[4,1024,256]{2,0,1:T(4,128)} dynamic-update-slice(f32[4,1024,256]{2,0,1:T(4,128)} %get-tuple-element.250, f32[1,1024,256]{2,0,1:T(1,128)} %copy.24, s32[]{:T(128)} %get-tuple-element.249, s32[]{:T(128)} %constant.3.clone.1..sunk, s32[]{:T(128)} %constant.3.clone.1..sunk) | dynamic-update-slice | bytes 2097156 | tf_op jit(solution)/shard_map/while/body/jit(dynamic_update_index_in_dim)/dynamic_update_slice | solution.py:57
  310.7 4.1 fusion.100
  315.8 2.5 fusion.102
  318.4 1.0 convolution_add_fusion.9
  319.4 2.5 fusion.103
  323.0 2.5 fusion.104
  326.5 3.7 fusion.105
  330.3 2.3 convolution_add_fusion.12
  332.5 3.7 fusion.106
  336.3 3.2 fusion.107
  339.5 3.6 copy.24
  343.1 23.2 %dynamic_update_slice.5 = f32[4,1024,256]{2,0,1:T(4,128)} dynamic-update-slice(f32[4,1024,256]{2,0,1:T(4,128)} %get-tuple-element.250, f32[1,1024,256]{2,0,1:T(1,128)} %copy.24, s32[]{:T(128)} %get-tuple-element.249, s32[]{:T(128)} %constant.3.clone.1..sunk, s32[]{:T(128)} %constant.3.clone.1..sunk) | dynamic-update-slice | bytes 2097156 | tf_op jit(solution)/shard_map/while/body/jit(dynamic_update_index_in_dim)/dynamic_update_slice | solution.py:57
  366.4 48.4 %all_to_all.36 = f32[4,1024,256]{2,0,1:T(4,128)S(1)} all-to-all(f32[4,1024,256]{2,0,1:T(4,128)} %get-tuple-element.92), channel_id=1, replica_groups=mesh['blk'=8,'vb'=4] {'vb'}, dimensions={1} | all-to-all | bytes 8388608 | tf_op jit(solution)/shard_map/all_to_all | solution.py:58
  414.8 4.7 %copy.18 = f32[4,256,4,256]{3,2,1,0:T(4,128)} copy(f32[4,256,4,256]{3,0,1,2:T(4,128)S(1)} %bitcast.132) | data formatting | bytes 8388608 | tf_op jit(solution)/shard_map/all_to_all | solution.py:58
  419.5 5.8 %all_to_all.33 = f32[4,256,1024]{2,1,0:T(8,128)} reshape(f32[4,256,4,256]{3,2,1,0:T(4,128)} %copy.18) | data formatting | bytes 8388608 | tf_op jit(solution)/shard_map/all_to_all | solution.py:58
  (58 shorter events, 16.7 us)
Async XLA Ops:
  0.0 26.4 %collective-permute-start = (f32[256,1024]{1,0:T(8,128)}, f32[256,1024]{1,0:T(8,128)S(1)}, u32[]{:S(2)}, u32[]{:S(2)}) collective-permute-start(f32[256,1024]{1,0:T(8,128)} %param.9), channel_id=1, source_target_pairs={{12,0},{16,4},{20,8},{24,12},{28,16},{0,20},{4,24},{8,28},{13,1},{... | collective-permute-start | bytes 3145736 | tf_op jit(solution)/shard_map/ppermute | solution.py:12
  26.4 28.4 %collective-permute-start.2 = (f32[256,1024]{1,0:T(8,128)S(1)}, f32[256,1024]{1,0:T(8,128)S(1)}, u32[]{:S(2)}, u32[]{:S(2)}) collective-permute-start(f32[256,1024]{1,0:T(8,128)S(1)} %collective-permute-done), channel_id=1, source_target_pairs={{28,0},{0,4},{4,8},{8,12},{12,16},{16,20},{20,24},{24,28},{29,1},{... | collective-permute-start | bytes 3145736 | tf_op jit(solution)/shard_map/ppermute | solution.py:12
  54.8 16.0 %collective-permute-start.4 = (f32[256,1024]{1,0:T(8,128)S(1)}, f32[256,1024]{1,0:T(8,128)S(1)}, u32[]{:S(2)}, u32[]{:S(2)}) collective-permute-start(f32[256,1024]{1,0:T(8,128)S(1)} %collective-permute-done.2), channel_id=1, source_target_pairs={{28,0},{0,4},{4,8},{8,12},{12,16},{16,20},{20,24},{24,28},{29,1},{... | collective-permute-start | bytes 3145736 | tf_op jit(solution)/shard_map/ppermute | solution.py:12
  60.1 44.0 %copy-start.3 = (f32[1024]{0:T(1024)S(1)}, f32[1024]{0:T(1024)}, u32[]{:S(2)}) copy-start(f32[1024]{0:T(1024)} %param.13) | copy-start | bytes 12292
  60.1 44.0 %copy-start.6 = (s32[256]{0:T(256)S(1)}, s32[256]{0:T(256)}, u32[]{:S(2)}) copy-start(s32[256]{0:T(256)} %param.10) | copy-start | bytes 3076
  60.1 75.2 %copy-start.4 = (f32[256]{0:T(256)S(1)}, f32[256]{0:T(256)}, u32[]{:S(2)}) copy-start(f32[256]{0:T(256)} %param.12) | copy-start | bytes 3076
  60.1 75.2 %copy-start.5 = (s32[4,2]{0,1:T(2,128)S(1)}, s32[4,2]{0,1:T(2,128)}, u32[]{:S(2)}) copy-start(s32[4,2]{0,1:T(2,128)} %param.11) | copy-start | bytes 100
  60.1 75.5 %all-to-all-start = ((f32[4,256,1024]{1,0,2:T(4,128)}), f32[4,256,1024]{1,0,2:T(4,128)}, u32[]{:S(2)}, u32[]{:S(2)}) async-start(f32[4,256,1024]{1,0,2:T(4,128)} %copy.15), calls=%async_computation | async-start | bytes 8388608 | tf_op jit(solution)/shard_map/all_to_all | solution.py:39
  70.8 16.0 %collective-permute-start.6 = (f32[256,1024]{1,0:T(8,128)S(1)}, f32[256,1024]{1,0:T(8,128)S(1)}, u32[]{:S(2)}, u32[]{:S(2)}) collective-permute-start(f32[256,1024]{1,0:T(8,128)S(1)} %collective-permute-done.4), channel_id=1, source_target_pairs={{28,0},{0,4},{4,8},{8,12},{12,16},{16,20},{20,24},{24,28},{29,1},{... | collective-permute-start | bytes 3145736 | tf_op jit(solution)/shard_map/ppermute | solution.py:12
  86.8 1.1 copy-start.1
  87.9 16.1 %collective-permute-start.8 = (f32[256,1024]{1,0:T(8,128)S(1)}, f32[256,1024]{1,0:T(8,128)}, u32[]{:S(2)}, u32[]{:S(2)}) collective-permute-start(f32[256,1024]{1,0:T(8,128)S(1)} %collective-permute-done.6), channel_id=1, source_target_pairs={{28,0},{0,4},{4,8},{8,12},{12,16},{16,20},{20,24},{24,28},{29,1},{... | collective-permute-start | bytes 3145736 | tf_op jit(solution)/shard_map/ppermute | solution.py:12
  104.0 36.8 %collective-permute-start.10 = (f32[256,1024]{1,0:T(8,128)}, f32[256,1024]{1,0:T(8,128)}, u32[]{:S(2)}, u32[]{:S(2)}) collective-permute-start(f32[256,1024]{1,0:T(8,128)} %collective-permute-done.8), channel_id=1, source_target_pairs={{28,0},{0,4},{4,8},{8,12},{12,16},{16,20},{20,24},{24,28},{29,1},{... | collective-permute-start | bytes 3145736 | tf_op jit(solution)/shard_map/ppermute | solution.py:12
  104.3 3.1 collective-permute-start.1
  107.4 13.5 %collective-permute-start.3 = (f32[256]{0:T(256)S(1)}, f32[256]{0:T(256)S(1)}, u32[]{:S(2)}, u32[]{:S(2)}) collective-permute-start(f32[256]{0:T(256)S(1)} %collective-permute-done.1), channel_id=1, source_target_pairs={{28,0},{0,4},{4,8},{8,12},{12,16},{16,20},{20,24},{24,28},{29,1},{... | collective-permute-start | bytes 3080 | tf_op jit(solution)/shard_map/ppermute | solution.py:12
  120.9 4.8 %collective-permute-start.5 = (f32[256]{0:T(256)S(1)}, f32[256]{0:T(256)S(1)}, u32[]{:S(2)}, u32[]{:S(2)}) collective-permute-start(f32[256]{0:T(256)S(1)} %collective-permute-done.3), channel_id=1, source_target_pairs={{28,0},{0,4},{4,8},{8,12},{12,16},{16,20},{20,24},{24,28},{29,1},{... | collective-permute-start | bytes 3080 | tf_op jit(solution)/shard_map/ppermute | solution.py:12
  125.7 4.8 %collective-permute-start.7 = (f32[256]{0:T(256)S(1)}, f32[256]{0:T(256)S(1)}, u32[]{:S(2)}, u32[]{:S(2)}) collective-permute-start(f32[256]{0:T(256)S(1)} %collective-permute-done.5), channel_id=1, source_target_pairs={{28,0},{0,4},{4,8},{8,12},{12,16},{16,20},{20,24},{24,28},{29,1},{... | collective-permute-start | bytes 3080 | tf_op jit(solution)/shard_map/ppermute | solution.py:12
  130.5 4.8 %collective-permute-start.9 = (f32[256]{0:T(256)S(1)}, f32[256]{0:T(256)S(1)}, u32[]{:S(2)}, u32[]{:S(2)}) collective-permute-start(f32[256]{0:T(256)S(1)} %collective-permute-done.7), channel_id=1, source_target_pairs={{28,0},{0,4},{4,8},{8,12},{12,16},{16,20},{20,24},{24,28},{29,1},{... | collective-permute-start | bytes 3080 | tf_op jit(solution)/shard_map/ppermute | solution.py:12
  135.3 5.5 %collective-permute-start.11 = (f32[256]{0:T(256)S(1)}, f32[256]{0:T(256)S(1)}, u32[]{:S(2)}, u32[]{:S(2)}) collective-permute-start(f32[256]{0:T(256)S(1)} %collective-permute-done.9), channel_id=1, source_target_pairs={{28,0},{0,4},{4,8},{8,12},{12,16},{16,20},{20,24},{24,28},{29,1},{... | collective-permute-start | bytes 3080 | tf_op jit(solution)/shard_map/ppermute | solution.py:12
  141.0 5.8 %copy-start = (f32[4,1024,256]{2,1,0:T(8,128)S(1)}, f32[4,1024,256]{2,1,0:T(8,128)}, u32[]{:S(2)}) copy-start(f32[4,1024,256]{2,1,0:T(8,128)} %get-tuple-element.270) | copy-start | bytes 12582916 | tf_op jit(solution)/shard_map/while
  149.3 4.6 %copy-start.2 = (f32[256,1024]{1,0:T(8,128)S(1)}, f32[256,1024]{1,0:T(8,128)}, u32[]{:S(2)}) copy-start(f32[256,1024]{1,0:T(8,128)} %get-tuple-element.279) | copy-start | bytes 3145732 | tf_op jit(solution)/shard_map/while
  197.4 5.8 %copy-start = (f32[4,1024,256]{2,1,0:T(8,128)S(1)}, f32[4,1024,256]{2,1,0:T(8,128)}, u32[]{:S(2)}) copy-start(f32[4,1024,256]{2,1,0:T(8,128)} %get-tuple-element.270) | copy-start | bytes 12582916 | tf_op jit(solution)/shard_map/while
  205.7 4.6 %copy-start.2 = (f32[256,1024]{1,0:T(8,128)S(1)}, f32[256,1024]{1,0:T(8,128)}, u32[]{:S(2)}) copy-start(f32[256,1024]{1,0:T(8,128)} %get-tuple-element.279) | copy-start | bytes 3145732 | tf_op jit(solution)/shard_map/while
  253.7 5.8 %copy-start = (f32[4,1024,256]{2,1,0:T(8,128)S(1)}, f32[4,1024,256]{2,1,0:T(8,128)}, u32[]{:S(2)}) copy-start(f32[4,1024,256]{2,1,0:T(8,128)} %get-tuple-element.270) | copy-start | bytes 12582916 | tf_op jit(solution)/shard_map/while
  262.0 4.6 %copy-start.2 = (f32[256,1024]{1,0:T(8,128)S(1)}, f32[256,1024]{1,0:T(8,128)}, u32[]{:S(2)}) copy-start(f32[256,1024]{1,0:T(8,128)} %get-tuple-element.279) | copy-start | bytes 3145732 | tf_op jit(solution)/shard_map/while
  310.1 5.8 %copy-start = (f32[4,1024,256]{2,1,0:T(8,128)S(1)}, f32[4,1024,256]{2,1,0:T(8,128)}, u32[]{:S(2)}) copy-start(f32[4,1024,256]{2,1,0:T(8,128)} %get-tuple-element.270) | copy-start | bytes 12582916 | tf_op jit(solution)/shard_map/while
  318.4 4.6 %copy-start.2 = (f32[256,1024]{1,0:T(8,128)S(1)}, f32[256,1024]{1,0:T(8,128)}, u32[]{:S(2)}) copy-start(f32[256,1024]{1,0:T(8,128)} %get-tuple-element.279) | copy-start | bytes 3145732 | tf_op jit(solution)/shard_map/while
where the time goes:
time: 429 us; the launch traced here: 425 us
  local copies, waits for them, and re-layouts  132 us (31%)
  matrix products  115 us (27%)
  waiting for transfers between devices  104 us (24%)
  blocking collectives  48.4 us (11%)
  starting transfers between devices  24.3 us (6%)
    dynamic_update_slice x8, local copies, waits for them, and re-layouts, local(): totals = lax.map(pair_columns, (factors, pair_energy))  107 us
    ppermute x12, waiting for transfers between devices, passed_along(): return lax.ppermute(block, axis, route)  104 us
    dot_general x24, matrix products, pair_columns(): jnp.dot(block, factor, precision=lax.Precision.HIGHEST, preferred_element...  76.2 us
    all_to_all x1, blocking collectives, local(): return lax.all_to_all(totals, 'vb', split_axis=1, concat_axis=2, tiled=True)  48.4 us
    dot_general x24, matrix products, pair_columns(): jnp.dot(block.T, weighted / denom, precision=lax.Precision.HIGHEST, prefe...  38.5 us
    ppermute x12, starting transfers between devices, passed_along(): return lax.ppermute(block, axis, route)  19.3 us
    all_to_all x2, local copies, waits for them, and re-layouts, local(): return lax.all_to_all(totals, 'vb', split_axis=1, concat_axis=2, tiled=True)  10.4 us
  transfers between devices with their start and end apart: 13, of which 10 were waited for; matrix products, arithmetic and copies ran while one was open for 3% of the time, Pallas kernels for 0%

commit v1 on v0

--- a/solution.py
+++ b/solution.py
@@ -1,9 +1,21 @@
+import functools
 import jax
 import jax.numpy as jnp
 from jax import lax
 from jax.sharding import PartitionSpec as P
 
 HOPS = 5
+
+
+def group_face_up(inner_x, group_axis, dimension_no, at_axis):
+    carry = lax.psum(1, group_axis)
+    extra = jnp.split(inner_x, carry, axis=dimension_no)
+    local_now = jnp.stack(extra)
+    vec_out = lax.all_to_all(local_now, group_axis, 0, 0)
+    return jnp.concatenate(vec_out, axis=at_axis)
+
+
+_set_sources_all = functools.partial(group_face_up, group_axis="vb", dimension_no=1, at_axis=2)
 
 
 def passed_along(block, axis, distance):
@@ -55,7 +67,7 @@
         return total
 
     totals = lax.map(pair_columns, (factors, pair_energy))
-    return lax.all_to_all(totals, "vb", split_axis=1, concat_axis=2, tiled=True)
+    return _set_sources_all(totals)
 
 
 def solution(mesh):

time: 429 us -> 321 us (0.75)
  local copies, waits for them, and re-layouts: 132 us -> 27.8 us
    dynamic_update_slice x8 -> x0, local copies, waits for them, and re-layouts: 107 us -> none  [local(): totals = lax.map(pair_columns, (factors, pair_energy))]
    reshape x0 -> x2, local copies, waits for them, and re-layouts: none -> 11.1 us  [group_face_up(): return jnp.concatenate(vec_out, axis=at_axis)]
    all_to_all x2 -> x0, local copies, waits for them, and re-layouts: 10.4 us -> none  [local(): return lax.all_to_all(totals, 'vb', split_axis=1, concat_axis=2, tiled=True)]
where the time goes in v1:
time: 321 us; the launch traced here: 319 us
  matrix products  113 us (35%)
  waiting for transfers between devices  104 us (32%)
  blocking collectives  48.1 us (15%)
  local copies, waits for them, and re-layouts  27.8 us (9%)
  starting transfers between devices  24.3 us (8%)
    ppermute x12, waiting for transfers between devices, passed_along(): return lax.ppermute(block, axis, route)  104 us
    dot_general x24, matrix products, pair_columns(): jnp.dot(block, factor, precision=lax.Precision.HIGHEST, preferred_element...  74.7 us
    all_to_all x1, blocking collectives, group_face_up(): vec_out = lax.all_to_all(local_now, group_axis, 0, 0)  48.1 us
    dot_general x24, matrix products, pair_columns(): jnp.dot(block.T, weighted / denom, precision=lax.Precision.HIGHEST, prefe...  38.5 us
    ppermute x12, starting transfers between devices, passed_along(): return lax.ppermute(block, axis, route)  19.3 us
    reshape x2, local copies, waits for them, and re-layouts, group_face_up(): return jnp.concatenate(vec_out, axis=at_axis)  11.1 us
  transfers between devices with their start and end apart: 13, of which 10 were waited for; matrix products, arithmetic and copies ran while one was open for 3% of the time, Pallas kernels for 0%

profile of v1, /device:TPU:0, one launch (start us, length us, event | category | flops | bytes accessed | tf_op | source)
XLA Modules:
  0.0 319.3 jit_solution(16279006392219111150)
XLA Ops:
  0.0 3.5 %collective-permute-start = (f32[256,1024]{1,0:T(8,128)}, f32[256,1024]{1,0:T(8,128)S(1)}, u32[]{:S(2)}, u32[]{:S(2)}) collective-permute-start(f32[256,1024]{1,0:T(8,128)} %param.9), channel_id=1, source_target_pairs={{12,0},{16,4},{20,8},{24,12},{28,16},{0,20},{4,24},{8,28},{13,1},{... | collective-permute-start | bytes 3145736 | tf_op jit(solution)/shard_map/ppermute | solution.py:24
  3.5 22.9 %collective-permute-done = f32[256,1024]{1,0:T(8,128)S(1)} collective-permute-done((f32[256,1024]{1,0:T(8,128)}, f32[256,1024]{1,0:T(8,128)S(1)}, u32[]{:S(2)}, u32[]{:S(2)}) %collective-permute-start) | collective-permute-done | bytes 1048608 | tf_op jit(solution)/shard_map/ppermute | solution.py:24
  26.4 12.8 %collective-permute-start.2 = (f32[256,1024]{1,0:T(8,128)S(1)}, f32[256,1024]{1,0:T(8,128)S(1)}, u32[]{:S(2)}, u32[]{:S(2)}) collective-permute-start(f32[256,1024]{1,0:T(8,128)S(1)} %collective-permute-done), channel_id=1, source_target_pairs={{28,0},{0,4},{4,8},{8,12},{12,16},{16,20},{20,24},{24,28},{29,1},{... | collective-permute-start | bytes 3145736 | tf_op jit(solution)/shard_map/ppermute | solution.py:24
  39.2 15.6 %collective-permute-done.2 = f32[256,1024]{1,0:T(8,128)S(1)} collective-permute-done((f32[256,1024]{1,0:T(8,128)S(1)}, f32[256,1024]{1,0:T(8,128)S(1)}, u32[]{:S(2)}, u32[]{:S(2)}) %collective-permute-start.2) | collective-permute-done | bytes 1048608 | tf_op jit(solution)/shard_map/ppermute | solution.py:24
  54.8 5.3 %copy.14 = f32[4,256,1024]{1,0,2:T(4,128)} copy(f32[4,256,1024]{2,1,0:T(8,128)} %param.8) | data formatting | bytes 8388608 | tf_op args[0]
  60.1 5.0 %all-to-all-start = ((f32[4,256,1024]{1,0,2:T(4,128)}), f32[4,256,1024]{1,0,2:T(4,128)}, u32[]{:S(2)}, u32[]{:S(2)}) async-start(f32[4,256,1024]{1,0,2:T(4,128)} %copy.14), calls=%async_computation | async-start | bytes 8388608 | tf_op jit(solution)/shard_map/all_to_all | solution.py:51
  65.1 5.7 %collective-permute-done.4 = f32[256,1024]{1,0:T(8,128)S(1)} collective-permute-done((f32[256,1024]{1,0:T(8,128)S(1)}, f32[256,1024]{1,0:T(8,128)S(1)}, u32[]{:S(2)}, u32[]{:S(2)}) %collective-permute-start.4) | collective-permute-done | bytes 1048608 | tf_op jit(solution)/shard_map/ppermute | solution.py:24
  70.8 16.0 %collective-permute-done.6 = f32[256,1024]{1,0:T(8,128)S(1)} collective-permute-done((f32[256,1024]{1,0:T(8,128)S(1)}, f32[256,1024]{1,0:T(8,128)S(1)}, u32[]{:S(2)}, u32[]{:S(2)}) %collective-permute-start.6) | collective-permute-done | bytes 1048608 | tf_op jit(solution)/shard_map/ppermute | solution.py:24
  86.8 1.0 copy-done.1
  87.9 16.1 %collective-permute-done.8 = f32[256,1024]{1,0:T(8,128)} collective-permute-done((f32[256,1024]{1,0:T(8,128)S(1)}, f32[256,1024]{1,0:T(8,128)}, u32[]{:S(2)}, u32[]{:S(2)}) %collective-permute-start.8) | collective-permute-done | bytes 1048608 | tf_op jit(solution)/shard_map/ppermute | solution.py:24
  104.4 3.0 collective-permute-done.1
  107.3 3.0 collective-permute-start.3
  110.3 10.6 %collective-permute-done.3 = f32[256]{0:T(256)S(1)} collective-permute-done((f32[256]{0:T(256)S(1)}, f32[256]{0:T(256)S(1)}, u32[]{:S(2)}, u32[]{:S(2)}) %collective-permute-start.3) | collective-permute-done | bytes 1056 | tf_op jit(solution)/shard_map/ppermute | solution.py:24
  120.9 4.8 %collective-permute-done.5 = f32[256]{0:T(256)S(1)} collective-permute-done((f32[256]{0:T(256)S(1)}, f32[256]{0:T(256)S(1)}, u32[]{:S(2)}, u32[]{:S(2)}) %collective-permute-start.5) | collective-permute-done | bytes 1056 | tf_op jit(solution)/shard_map/ppermute | solution.py:24
  125.7 4.8 %collective-permute-done.7 = f32[256]{0:T(256)S(1)} collective-permute-done((f32[256]{0:T(256)S(1)}, f32[256]{0:T(256)S(1)}, u32[]{:S(2)}, u32[]{:S(2)}) %collective-permute-start.7) | collective-permute-done | bytes 1056 | tf_op jit(solution)/shard_map/ppermute | solution.py:24
  130.5 4.8 %collective-permute-done.9 = f32[256]{0:T(256)S(1)} collective-permute-done((f32[256]{0:T(256)S(1)}, f32[256]{0:T(256)S(1)}, u32[]{:S(2)}, u32[]{:S(2)}) %collective-permute-start.9) | collective-permute-done | bytes 1056 | tf_op jit(solution)/shard_map/ppermute | solution.py:24
  135.6 5.2 %copy.15 = f32[4,4,256,256]{3,2,1,0:T(8,128)} copy(f32[4,4,256,256]{2,0,3,1:T(4,128)} %bitcast.11) | data formatting | bytes 8388608 | tf_op jit(solution)/shard_map/all_to_all | solution.py:51
  140.8 116.3 %while.10 = (s32[]{:T(128)}, f32[4,1024,256]{1,2,0:T(8,128)}, f32[4,1024,256]{2,1,0:T(8,128)}, f32[256,1024]{1,0:T(8,128)S(1)}, f32[256]{0:T(256)S(1)}, /*index=...) while((s32[]{:T(128)}, f32[4,1024,256]{1,2,0:T(8,128)}, ...), condition=%wide.region_3.4_spmd, body=%wide.region_2.3_spmd.sunk | while | flops 9666166784 | bytes 54540048 | solution.py:69
  141.6 4.0 %fusion.101 = f32[256,256]{0,1:T(8,128)S(1)} fusion(f32[256,1024]{1,0:T(8,128)S(1)} %get-tuple-element.273, f32[4,1024,256]{2,1,0:T(8,128)} %get-tuple-element.272, s32[]{:T(128)} %get-tuple-element.252, f32[]{:T(128)} %bitcast.138, f32[256]{0:T(256)S(1)} %get-tuple-element.275, f32[256]{0:T(256)S(1)} %get-tuple-element.274), kind=kOutput, calls=%fused_computation.18.clone.1 | convolution fusion | flops 805502976 | bytes 2362368 | tf_op jit(solution)/shard_map/while/body/eval_jaxpr/dot_general | solution.py:58
  146.7 2.4 fusion.103
  149.1 1.0 convolution_add_fusion.9
  150.2 2.5 fusion.104
  152.6 1.0 convolution_add_fusion.10
  153.7 2.5 fusion.105
  156.2 1.0 convolution_add_fusion.11
  157.2 3.7 %fusion.106 = f32[256,256]{0,1:T(8,128)S(1)} fusion(f32[256,1024]{1,0:T(8,128)} %get-tuple-element.283, f32[4,1024,256]{2,1,0:T(8,128)S(1)} %copy-done, s32[]{:T(128)} %get-tuple-element.252, f32[256]{0:T(256)S(1)} %get-tuple-element.284, f32[]{:T(128)} %bitcast.138, f32[256]{0:T(256)S(1)} %get-tuple-element.275), kind=kOutput, calls=%fused_computation.10.clone.1 | convolution fusion | flops 805502976 | bytes 2361352 | tf_op jit(solution)/shard_map/while/body/eval_jaxpr/dot_general | solution.py:58
  160.9 2.3 convolution_add_fusion.12
  163.1 3.7 %fusion.107 = f32[256,256]{0,1:T(8,128)S(1)} fusion(f32[256,1024]{1,0:T(8,128)} %get-tuple-element.285, f32[4,1024,256]{2,1,0:T(8,128)S(1)} %copy-done, s32[]{:T(128)} %get-tuple-element.252, f32[256]{0:T(256)S(1)} %get-tuple-element.286, f32[]{:T(128)} %bitcast.138, f32[256]{0:T(256)S(1)} %get-tuple-element.275), kind=kOutput, calls=%fused_computation.8.clone.1 | convolution fusion | flops 805502976 | bytes 2361352 | tf_op jit(solution)/shard_map/while/body/eval_jaxpr/dot_general | solution.py:58
  166.8 3.2 %fusion.108 = f32[4,1024,256]{1,2,0:T(8,128)} fusion(f32[4,1024,256]{1,2,0:T(8,128)} %get-tuple-element.253, s32[]{:T(128)} %get-tuple-element.252, f32[256,1024]{1,0:T(8,128)S(1)} %convolution_add_fusion.12, f32[256,256]{0,1:T(8,128)S(1)} %fusion.107, f32[256,1024]{1,0:T(8,128)} %get-tuple-element.285), kind=kOutput, calls=%fused_computation.2.clone.1 | convolution fusion | flops 805568512 | bytes 3408384 | tf_op jit(solution)/shard_map/while/body/eval_jaxpr/dot_general | solution.py:61
  170.7 4.0 %fusion.101 = f32[256,256]{0,1:T(8,128)S(1)} fusion(f32[256,1024]{1,0:T(8,128)S(1)} %get-tuple-element.273, f32[4,1024,256]{2,1,0:T(8,128)} %get-tuple-element.272, s32[]{:T(128)} %get-tuple-element.252, f32[]{:T(128)} %bitcast.138, f32[256]{0:T(256)S(1)} %get-tuple-element.275, f32[256]{0:T(256)S(1)} %get-tuple-element.274), kind=kOutput, calls=%fused_computation.18.clone.1 | convolution fusion | flops 805502976 | bytes 2362368 | tf_op jit(solution)/shard_map/while/body/eval_jaxpr/dot_general | solution.py:58
  175.7 2.4 fusion.103
  179.2 2.5 fusion.104
  181.7 1.0 convolution_add_fusion.10
  182.7 2.5 fusion.105
  185.2 1.0 convolution_add_fusion.11
  186.2 3.7 %fusion.106 = f32[256,256]{0,1:T(8,128)S(1)} fusion(f32[256,1024]{1,0:T(8,128)} %get-tuple-element.283, f32[4,1024,256]{2,1,0:T(8,128)S(1)} %copy-done, s32[]{:T(128)} %get-tuple-element.252, f32[256]{0:T(256)S(1)} %get-tuple-element.284, f32[]{:T(128)} %bitcast.138, f32[256]{0:T(256)S(1)} %get-tuple-element.275), kind=kOutput, calls=%fused_computation.10.clone.1 | convolution fusion | flops 805502976 | bytes 2361352 | tf_op jit(solution)/shard_map/while/body/eval_jaxpr/dot_general | solution.py:58
  189.9 2.3 convolution_add_fusion.12
  192.2 3.7 %fusion.107 = f32[256,256]{0,1:T(8,128)S(1)} fusion(f32[256,1024]{1,0:T(8,128)} %get-tuple-element.285, f32[4,1024,256]{2,1,0:T(8,128)S(1)} %copy-done, s32[]{:T(128)} %get-tuple-element.252, f32[256]{0:T(256)S(1)} %get-tuple-element.286, f32[]{:T(128)} %bitcast.138, f32[256]{0:T(256)S(1)} %get-tuple-element.275), kind=kOutput, calls=%fused_computation.8.clone.1 | convolution fusion | flops 805502976 | bytes 2361352 | tf_op jit(solution)/shard_map/while/body/eval_jaxpr/dot_general | solution.py:58
  195.8 3.2 %fusion.108 = f32[4,1024,256]{1,2,0:T(8,128)} fusion(f32[4,1024,256]{1,2,0:T(8,128)} %get-tuple-element.253, s32[]{:T(128)} %get-tuple-element.252, f32[256,1024]{1,0:T(8,128)S(1)} %convolution_add_fusion.12, f32[256,256]{0,1:T(8,128)S(1)} %fusion.107, f32[256,1024]{1,0:T(8,128)} %get-tuple-element.285), kind=kOutput, calls=%fused_computation.2.clone.1 | convolution fusion | flops 805568512 | bytes 3408384 | tf_op jit(solution)/shard_map/while/body/eval_jaxpr/dot_general | solution.py:61
  199.7 4.0 %fusion.101 = f32[256,256]{0,1:T(8,128)S(1)} fusion(f32[256,1024]{1,0:T(8,128)S(1)} %get-tuple-element.273, f32[4,1024,256]{2,1,0:T(8,128)} %get-tuple-element.272, s32[]{:T(128)} %get-tuple-element.252, f32[]{:T(128)} %bitcast.138, f32[256]{0:T(256)S(1)} %get-tuple-element.275, f32[256]{0:T(256)S(1)} %get-tuple-element.274), kind=kOutput, calls=%fused_computation.18.clone.1 | convolution fusion | flops 805502976 | bytes 2362368 | tf_op jit(solution)/shard_map/while/body/eval_jaxpr/dot_general | solution.py:58
  204.7 2.4 fusion.103
  207.2 1.0 convolution_add_fusion.9
  208.2 2.5 fusion.104
  210.7 1.0 convolution_add_fusion.10
  211.8 2.5 fusion.105
  214.2 1.0 convolution_add_fusion.11
  215.3 3.7 %fusion.106 = f32[256,256]{0,1:T(8,128)S(1)} fusion(f32[256,1024]{1,0:T(8,128)} %get-tuple-element.283, f32[4,1024,256]{2,1,0:T(8,128)S(1)} %copy-done, s32[]{:T(128)} %get-tuple-element.252, f32[256]{0:T(256)S(1)} %get-tuple-element.284, f32[]{:T(128)} %bitcast.138, f32[256]{0:T(256)S(1)} %get-tuple-element.275), kind=kOutput, calls=%fused_computation.10.clone.1 | convolution fusion | flops 805502976 | bytes 2361352 | tf_op jit(solution)/shard_map/while/body/eval_jaxpr/dot_general | solution.py:58
  218.9 2.3 convolution_add_fusion.12
  221.2 3.7 %fusion.107 = f32[256,256]{0,1:T(8,128)S(1)} fusion(f32[256,1024]{1,0:T(8,128)} %get-tuple-element.285, f32[4,1024,256]{2,1,0:T(8,128)S(1)} %copy-done, s32[]{:T(128)} %get-tuple-element.252, f32[256]{0:T(256)S(1)} %get-tuple-element.286, f32[]{:T(128)} %bitcast.138, f32[256]{0:T(256)S(1)} %get-tuple-element.275), kind=kOutput, calls=%fused_computation.8.clone.1 | convolution fusion | flops 805502976 | bytes 2361352 | tf_op jit(solution)/shard_map/while/body/eval_jaxpr/dot_general | solution.py:58
  224.9 3.2 %fusion.108 = f32[4,1024,256]{1,2,0:T(8,128)} fusion(f32[4,1024,256]{1,2,0:T(8,128)} %get-tuple-element.253, s32[]{:T(128)} %get-tuple-element.252, f32[256,1024]{1,0:T(8,128)S(1)} %convolution_add_fusion.12, f32[256,256]{0,1:T(8,128)S(1)} %fusion.107, f32[256,1024]{1,0:T(8,128)} %get-tuple-element.285), kind=kOutput, calls=%fused_computation.2.clone.1 | convolution fusion | flops 805568512 | bytes 3408384 | tf_op jit(solution)/shard_map/while/body/eval_jaxpr/dot_general | solution.py:61
  228.7 4.0 %fusion.101 = f32[256,256]{0,1:T(8,128)S(1)} fusion(f32[256,1024]{1,0:T(8,128)S(1)} %get-tuple-element.273, f32[4,1024,256]{2,1,0:T(8,128)} %get-tuple-element.272, s32[]{:T(128)} %get-tuple-element.252, f32[]{:T(128)} %bitcast.138, f32[256]{0:T(256)S(1)} %get-tuple-element.275, f32[256]{0:T(256)S(1)} %get-tuple-element.274), kind=kOutput, calls=%fused_computation.18.clone.1 | convolution fusion | flops 805502976 | bytes 2362368 | tf_op jit(solution)/shard_map/while/body/eval_jaxpr/dot_general | solution.py:58
  233.8 2.4 fusion.103
  237.3 2.5 fusion.104
  239.7 1.0 convolution_add_fusion.10
  240.8 2.5 fusion.105
  243.2 1.0 convolution_add_fusion.11
  244.3 3.7 %fusion.106 = f32[256,256]{0,1:T(8,128)S(1)} fusion(f32[256,1024]{1,0:T(8,128)} %get-tuple-element.283, f32[4,1024,256]{2,1,0:T(8,128)S(1)} %copy-done, s32[]{:T(128)} %get-tuple-element.252, f32[256]{0:T(256)S(1)} %get-tuple-element.284, f32[]{:T(128)} %bitcast.138, f32[256]{0:T(256)S(1)} %get-tuple-element.275), kind=kOutput, calls=%fused_computation.10.clone.1 | convolution fusion | flops 805502976 | bytes 2361352 | tf_op jit(solution)/shard_map/while/body/eval_jaxpr/dot_general | solution.py:58
  248.0 2.3 convolution_add_fusion.12
  250.2 3.7 %fusion.107 = f32[256,256]{0,1:T(8,128)S(1)} fusion(f32[256,1024]{1,0:T(8,128)} %get-tuple-element.285, f32[4,1024,256]{2,1,0:T(8,128)S(1)} %copy-done, s32[]{:T(128)} %get-tuple-element.252, f32[256]{0:T(256)S(1)} %get-tuple-element.286, f32[]{:T(128)} %bitcast.138, f32[256]{0:T(256)S(1)} %get-tuple-element.275), kind=kOutput, calls=%fused_computation.8.clone.1 | convolution fusion | flops 805502976 | bytes 2361352 | tf_op jit(solution)/shard_map/while/body/eval_jaxpr/dot_general | solution.py:58
  253.9 3.2 %fusion.108 = f32[4,1024,256]{1,2,0:T(8,128)} fusion(f32[4,1024,256]{1,2,0:T(8,128)} %get-tuple-element.253, s32[]{:T(128)} %get-tuple-element.252, f32[256,1024]{1,0:T(8,128)S(1)} %convolution_add_fusion.12, f32[256,256]{0,1:T(8,128)S(1)} %fusion.107, f32[256,1024]{1,0:T(8,128)} %get-tuple-element.285), kind=kOutput, calls=%fused_computation.2.clone.1 | convolution fusion | flops 805568512 | bytes 3408384 | tf_op jit(solution)/shard_map/while/body/eval_jaxpr/dot_general | solution.py:61
  257.1 2.6 slice_bitcast_fusion.3
  260.2 48.1 %all_to_all.23 = f32[4,4,256,256]{2,3,1,0:T(8,128)} all-to-all(f32[4,4,256,256]{2,3,1,0:T(8,128)S(1)} %pad_maximum_fusion), channel_id=1, replica_groups=mesh['blk'=8,'vb'=4] {'vb'}, dimensions={0} | all-to-all | bytes 8388608 | tf_op jit(solution)/shard_map/all_to_all | solution.py:14
  308.2 5.3 %copy.16 = f32[4,256,4,256]{3,2,1,0:T(4,128)} copy(f32[4,256,4,256]{1,3,0,2:T(8,128)} %bitcast.140) | data formatting | bytes 8388608 | tf_op jit(solution)/shard_map/reshape | solution.py:15
  313.5 5.8 %reshape.18 = f32[4,256,1024]{2,1,0:T(8,128)} reshape(f32[4,256,4,256]{3,2,1,0:T(4,128)} %copy.16) | data formatting | bytes 8388608 | tf_op jit(solution)/shard_map/reshape | solution.py:15
  (52 shorter events, 9.7 us)
Async XLA Ops:
  0.0 26.4 %collective-permute-start = (f32[256,1024]{1,0:T(8,128)}, f32[256,1024]{1,0:T(8,128)S(1)}, u32[]{:S(2)}, u32[]{:S(2)}) collective-permute-start(f32[256,1024]{1,0:T(8,128)} %param.9), channel_id=1, source_target_pairs={{12,0},{16,4},{20,8},{24,12},{28,16},{0,20},{4,24},{8,28},{13,1},{... | collective-permute-start | bytes 3145736 | tf_op jit(solution)/shard_map/ppermute | solution.py:24
  26.4 28.4 %collective-permute-start.2 = (f32[256,1024]{1,0:T(8,128)S(1)}, f32[256,1024]{1,0:T(8,128)S(1)}, u32[]{:S(2)}, u32[]{:S(2)}) collective-permute-start(f32[256,1024]{1,0:T(8,128)S(1)} %collective-permute-done), channel_id=1, source_target_pairs={{28,0},{0,4},{4,8},{8,12},{12,16},{16,20},{20,24},{24,28},{29,1},{... | collective-permute-start | bytes 3145736 | tf_op jit(solution)/shard_map/ppermute | solution.py:24
  54.8 16.0 %collective-permute-start.4 = (f32[256,1024]{1,0:T(8,128)S(1)}, f32[256,1024]{1,0:T(8,128)S(1)}, u32[]{:S(2)}, u32[]{:S(2)}) collective-permute-start(f32[256,1024]{1,0:T(8,128)S(1)} %collective-permute-done.2), channel_id=1, source_target_pairs={{28,0},{0,4},{4,8},{8,12},{12,16},{16,20},{20,24},{24,28},{29,1},{... | collective-permute-start | bytes 3145736 | tf_op jit(solution)/shard_map/ppermute | solution.py:24
  60.1 44.0 %copy-start.3 = (f32[1024]{0:T(1024)S(1)}, f32[1024]{0:T(1024)}, u32[]{:S(2)}) copy-start(f32[1024]{0:T(1024)} %param.13) | copy-start | bytes 12292
  60.1 44.0 %copy-start.6 = (s32[256]{0:T(256)S(1)}, s32[256]{0:T(256)}, u32[]{:S(2)}) copy-start(s32[256]{0:T(256)} %param.10) | copy-start | bytes 3076
  60.1 75.2 %copy-start.4 = (f32[256]{0:T(256)S(1)}, f32[256]{0:T(256)}, u32[]{:S(2)}) copy-start(f32[256]{0:T(256)} %param.12) | copy-start | bytes 3076
  60.1 75.2 %copy-start.5 = (s32[4,2]{0,1:T(2,128)S(1)}, s32[4,2]{0,1:T(2,128)}, u32[]{:S(2)}) copy-start(s32[4,2]{0,1:T(2,128)} %param.11) | copy-start | bytes 100
  60.1 75.5 %all-to-all-start = ((f32[4,256,1024]{1,0,2:T(4,128)}), f32[4,256,1024]{1,0,2:T(4,128)}, u32[]{:S(2)}, u32[]{:S(2)}) async-start(f32[4,256,1024]{1,0,2:T(4,128)} %copy.14), calls=%async_computation | async-start | bytes 8388608 | tf_op jit(solution)/shard_map/all_to_all | solution.py:51
  70.8 16.0 %collective-permute-start.6 = (f32[256,1024]{1,0:T(8,128)S(1)}, f32[256,1024]{1,0:T(8,128)S(1)}, u32[]{:S(2)}, u32[]{:S(2)}) collective-permute-start(f32[256,1024]{1,0:T(8,128)S(1)} %collective-permute-done.4), channel_id=1, source_target_pairs={{28,0},{0,4},{4,8},{8,12},{12,16},{16,20},{20,24},{24,28},{29,1},{... | collective-permute-start | bytes 3145736 | tf_op jit(solution)/shard_map/ppermute | solution.py:24
  86.8 1.1 copy-start.1
  87.9 16.1 %collective-permute-start.8 = (f32[256,1024]{1,0:T(8,128)S(1)}, f32[256,1024]{1,0:T(8,128)}, u32[]{:S(2)}, u32[]{:S(2)}) collective-permute-start(f32[256,1024]{1,0:T(8,128)S(1)} %collective-permute-done.6), channel_id=1, source_target_pairs={{28,0},{0,4},{4,8},{8,12},{12,16},{16,20},{20,24},{24,28},{29,1},{... | collective-permute-start | bytes 3145736 | tf_op jit(solution)/shard_map/ppermute | solution.py:24
  104.0 36.8 %collective-permute-start.10 = (f32[256,1024]{1,0:T(8,128)}, f32[256,1024]{1,0:T(8,128)}, u32[]{:S(2)}, u32[]{:S(2)}) collective-permute-start(f32[256,1024]{1,0:T(8,128)} %collective-permute-done.8), channel_id=1, source_target_pairs={{28,0},{0,4},{4,8},{8,12},{12,16},{16,20},{20,24},{24,28},{29,1},{... | collective-permute-start | bytes 3145736 | tf_op jit(solution)/shard_map/ppermute | solution.py:24
  104.3 3.1 collective-permute-start.1
  107.3 13.5 %collective-permute-start.3 = (f32[256]{0:T(256)S(1)}, f32[256]{0:T(256)S(1)}, u32[]{:S(2)}, u32[]{:S(2)}) collective-permute-start(f32[256]{0:T(256)S(1)} %collective-permute-done.1), channel_id=1, source_target_pairs={{28,0},{0,4},{4,8},{8,12},{12,16},{16,20},{20,24},{24,28},{29,1},{... | collective-permute-start | bytes 3080 | tf_op jit(solution)/shard_map/ppermute | solution.py:24
  120.9 4.8 %collective-permute-start.5 = (f32[256]{0:T(256)S(1)}, f32[256]{0:T(256)S(1)}, u32[]{:S(2)}, u32[]{:S(2)}) collective-permute-start(f32[256]{0:T(256)S(1)} %collective-permute-done.3), channel_id=1, source_target_pairs={{28,0},{0,4},{4,8},{8,12},{12,16},{16,20},{20,24},{24,28},{29,1},{... | collective-permute-start | bytes 3080 | tf_op jit(solution)/shard_map/ppermute | solution.py:24
  125.7 4.8 %collective-permute-start.7 = (f32[256]{0:T(256)S(1)}, f32[256]{0:T(256)S(1)}, u32[]{:S(2)}, u32[]{:S(2)}) collective-permute-start(f32[256]{0:T(256)S(1)} %collective-permute-done.5), channel_id=1, source_target_pairs={{28,0},{0,4},{4,8},{8,12},{12,16},{16,20},{20,24},{24,28},{29,1},{... | collective-permute-start | bytes 3080 | tf_op jit(solution)/shard_map/ppermute | solution.py:24
  130.5 4.8 %collective-permute-start.9 = (f32[256]{0:T(256)S(1)}, f32[256]{0:T(256)S(1)}, u32[]{:S(2)}, u32[]{:S(2)}) collective-permute-start(f32[256]{0:T(256)S(1)} %collective-permute-done.7), channel_id=1, source_target_pairs={{28,0},{0,4},{4,8},{8,12},{12,16},{16,20},{20,24},{24,28},{29,1},{... | collective-permute-start | bytes 3080 | tf_op jit(solution)/shard_map/ppermute | solution.py:24
  135.3 5.5 %collective-permute-start.11 = (f32[256]{0:T(256)S(1)}, f32[256]{0:T(256)S(1)}, u32[]{:S(2)}, u32[]{:S(2)}) collective-permute-start(f32[256]{0:T(256)S(1)} %collective-permute-done.9), channel_id=1, source_target_pairs={{28,0},{0,4},{4,8},{8,12},{12,16},{16,20},{20,24},{24,28},{29,1},{... | collective-permute-start | bytes 3080 | tf_op jit(solution)/shard_map/ppermute | solution.py:24
  141.0 5.7 %copy-start = (f32[4,1024,256]{2,1,0:T(8,128)S(1)}, f32[4,1024,256]{2,1,0:T(8,128)}, u32[]{:S(2)}) copy-start(f32[4,1024,256]{2,1,0:T(8,128)} %get-tuple-element.272) | copy-start | bytes 12582916 | tf_op jit(solution)/shard_map/while
  149.1 4.6 %copy-start.2 = (f32[256,1024]{1,0:T(8,128)S(1)}, f32[256,1024]{1,0:T(8,128)}, u32[]{:S(2)}) copy-start(f32[256,1024]{1,0:T(8,128)} %get-tuple-element.281) | copy-start | bytes 3145732 | tf_op jit(solution)/shard_map/while
  170.1 5.6 %copy-start = (f32[4,1024,256]{2,1,0:T(8,128)S(1)}, f32[4,1024,256]{2,1,0:T(8,128)}, u32[]{:S(2)}) copy-start(f32[4,1024,256]{2,1,0:T(8,128)} %get-tuple-element.272) | copy-start | bytes 12582916 | tf_op jit(solution)/shard_map/while
  178.2 4.6 %copy-start.2 = (f32[256,1024]{1,0:T(8,128)S(1)}, f32[256,1024]{1,0:T(8,128)}, u32[]{:S(2)}) copy-start(f32[256,1024]{1,0:T(8,128)} %get-tuple-element.281) | copy-start | bytes 3145732 | tf_op jit(solution)/shard_map/while
  199.1 5.6 %copy-start = (f32[4,1024,256]{2,1,0:T(8,128)S(1)}, f32[4,1024,256]{2,1,0:T(8,128)}, u32[]{:S(2)}) copy-start(f32[4,1024,256]{2,1,0:T(8,128)} %get-tuple-element.272) | copy-start | bytes 12582916 | tf_op jit(solution)/shard_map/while
  207.2 4.6 %copy-start.2 = (f32[256,1024]{1,0:T(8,128)S(1)}, f32[256,1024]{1,0:T(8,128)}, u32[]{:S(2)}) copy-start(f32[256,1024]{1,0:T(8,128)} %get-tuple-element.281) | copy-start | bytes 3145732 | tf_op jit(solution)/shard_map/while
  228.1 5.6 %copy-start = (f32[4,1024,256]{2,1,0:T(8,128)S(1)}, f32[4,1024,256]{2,1,0:T(8,128)}, u32[]{:S(2)}) copy-start(f32[4,1024,256]{2,1,0:T(8,128)} %get-tuple-element.272) | copy-start | bytes 12582916 | tf_op jit(solution)/shard_map/while
  236.2 4.6 %copy-start.2 = (f32[256,1024]{1,0:T(8,128)S(1)}, f32[256,1024]{1,0:T(8,128)}, u32[]{:S(2)}) copy-start(f32[256,1024]{1,0:T(8,128)} %get-tuple-element.281) | copy-start | bytes 3145732 | tf_op jit(solution)/shard_map/while
